TPU v7x, 256 devices: a whole 4x4x8 slice. The times are simulated.
256 devices in a mesh: expert: 64 (over y, z, core), tensor: 4 (over x).
Axes of the slice: x: 4, y: 4, z: 8, core: 2. Of those that a mesh axis runs over, the one named last changes fastest.
Arguments:
- tokens: bfloat16 [8192, 2048], P('expert', 'tensor'), may hold values from -6 to 6
- labels: int32 [8192, 1], P('expert'), may hold values from 0 to 31, as said below
- domain_ids: int32 [8192], P('expert'), may hold values from 0 to 21
- domain_weights: float32 [22], replicated, may hold values from 0.02 to 0.5
- cotangent: bfloat16 [8192, 2048], P('expert', 'tensor'), may hold values from -6 to 6
- gate_weight: bfloat16 [64, 2048, 2048], P('expert', None, 'tensor'), may hold values from -0.125 to 0.125
- up_weight: bfloat16 [64, 2048, 2048], P('expert', None, 'tensor'), may hold values from -0.125 to 0.125
- down_weight: bfloat16 [64, 2048, 2048], P('expert', 'tensor'), may hold values from -0.09375 to 0.09375
Outputs:
- layer_out: bfloat16 [8192, 2048], P('expert', 'tensor')
- input_grad: bfloat16 [8192, 2048], P('expert', 'tensor')
- gate_grad: bfloat16 [64, 2048, 2048], P('expert', None, 'tensor')
- up_grad: bfloat16 [64, 2048, 2048], P('expert', None, 'tensor')
- down_grad: bfloat16 [64, 2048, 2048], P('expert', 'tensor')
Inputs may be any that keep to these rules, and one draw needn't show every extreme that they name: `labels`: among the rows of one device (aligned blocks of 128 rows) no label appears more than 8 times, and every such block has some label exactly 8 times.
All inputs are finite; a program needn't handle non-finite values.
Results may differ from a plain program's by a relative error of at most 0.0058.
Values may be sent and summed in bfloat16 or wider, within the bound.
No kernel may reach another device: no remote copies, remote signals or barrier semaphores. Data moves between devices by JAX's collectives and lax.ppermute only.
A program may use at most 320 MiB of HBM per device.

v0:
```python
import jax
import jax.numpy as jnp
from jax import lax
from jax.sharding import PartitionSpec as P

SPLIT = 2


def partner(value, axis, stride):
    return lax.ppermute(value, axis, [(i, i ^ 1 << stride) for i in range(lax.axis_size(axis))])


def silu_parts(gate_pre):
    squash = jax.nn.sigmoid(gate_pre)
    return (squash, gate_pre * squash)


def body(
    tokens, labels, domain_ids, domain_weights, cotangent, gate_weight, up_weight, down_weight
):
    n_expert = lax.axis_size("expert")
    tok_rows = tokens.shape[0]
    experts_all = n_expert // SPLIT
    capacity = 2 * tok_rows // experts_all
    half_cap = capacity // 2
    parity = lax.axis_index("expert") % 2
    lang_label = labels[:, 0]
    dom_hot = (
        domain_ids[:, None] == jnp.arange(domain_weights.shape[0], dtype=jnp.int32)[None, :]
    ).astype(jnp.float32)
    tok_scale = jnp.sum(dom_hot * domain_weights[None, :], axis=1)
    grad_rows = (tok_scale[:, None] * cotangent.astype(jnp.float32)).astype(jnp.bfloat16)
    lab_hot = (lang_label[:, None] == jnp.arange(experts_all, dtype=jnp.int32)[None, :]).astype(
        jnp.float32
    )
    row_ids = jnp.arange(tok_rows, dtype=jnp.int32)
    earlier = (row_ids[None, :] < row_ids[:, None]).astype(jnp.float32)
    before = jnp.dot(earlier, lab_hot, precision=lax.Precision.HIGHEST)
    slot_pos = jnp.sum(before * lab_hot, axis=1).astype(jnp.int32)
    target_row = lang_label * capacity + slot_pos
    sources = jnp.stack((tokens, grad_rows))
    sources = lax.all_gather(sources, "tensor", axis=2, tiled=True)
    slot_ids = jnp.arange(n_expert * capacity, dtype=jnp.int32)
    dispatch_map = (slot_ids[:, None] // capacity // SPLIT == lang_label[None, :]) & (
        slot_ids[:, None] % capacity == slot_pos[None, :]
    )
    dispatch_map = dispatch_map.astype(jnp.bfloat16)
    outbound = jnp.einsum(
        "rt,ktw->krw", dispatch_map, sources, preferred_element_type=jnp.float32
    ).astype(jnp.bfloat16)
    outbound = outbound.reshape(2, n_expert, capacity, sources.shape[2])
    arrived = lax.all_to_all(outbound, "expert", split_axis=1, concat_axis=1, tiled=True)
    rows_all = n_expert * capacity
    feat_width = arrived.shape[3]
    routed = arrived[0].reshape(rows_all, feat_width)
    routed_grad = arrived[1].reshape(rows_all, feat_width)
    w_gate = gate_weight[0]
    w_up = up_weight[0]
    w_down = down_weight[0]
    contract_rows = (((0,), (0,)), ((), ()))
    contract_cols = (((1,), (1,)), ((), ()))
    gate_pre = jnp.dot(routed, w_gate, preferred_element_type=jnp.float32)
    up_pre = jnp.dot(routed, w_up, preferred_element_type=jnp.float32)
    squash, activated = silu_parts(gate_pre)
    hidden = (activated * up_pre).astype(jnp.bfloat16)
    out_part = jnp.dot(hidden, w_down, preferred_element_type=jnp.float32)
    grad_hidden = lax.dot_general(
        routed_grad, w_down, contract_cols, preferred_element_type=jnp.float32
    )
    grad_gate_pre = (grad_hidden * up_pre * squash * (1.0 + gate_pre * (1.0 - squash))).astype(
        jnp.bfloat16
    )
    grad_up_pre = (grad_hidden * activated).astype(jnp.bfloat16)
    gate_grad = lax.dot_general(
        routed, grad_gate_pre, contract_rows, preferred_element_type=jnp.float32
    ).astype(jnp.bfloat16)[None]
    up_grad = lax.dot_general(
        routed, grad_up_pre, contract_rows, preferred_element_type=jnp.float32
    ).astype(jnp.bfloat16)[None]
    down_grad = lax.dot_general(
        hidden, routed_grad, contract_rows, preferred_element_type=jnp.float32
    ).astype(jnp.bfloat16)[None]
    input_part = lax.dot_general(
        grad_gate_pre, w_gate, contract_cols, preferred_element_type=jnp.float32
    ) + lax.dot_general(grad_up_pre, w_up, contract_cols, preferred_element_type=jnp.float32)
    out_part = out_part.reshape(n_expert, capacity, feat_width)
    input_part = input_part.reshape(n_expert, capacity, feat_width)
    out_share, input_share = (
        lax.psum_scatter(out_part, "tensor", scatter_dimension=2, tiled=True),
        lax.psum_scatter(input_part, "tensor", scatter_dimension=2, tiled=True),
    )
    partial_value = jnp.stack((out_share, input_share))
    kept = jnp.where(parity == 0, partial_value[:, :, :half_cap], partial_value[:, :, half_cap:])
    handed = jnp.where(parity == 0, partial_value[:, :, half_cap:], partial_value[:, :, :half_cap])
    summed = kept + partner(handed, "expert", 0)
    going_back = summed.astype(jnp.bfloat16)
    returned = lax.all_to_all(going_back, "expert", split_axis=1, concat_axis=1, tiled=True)
    home_ids = jnp.arange(n_expert * half_cap, dtype=jnp.int32)
    home_map = (home_ids[:, None] == target_row[None, :]).astype(jnp.bfloat16)
    flat_back = returned.reshape(2, n_expert * half_cap, returned.shape[3])
    gathered_home = jnp.einsum(
        "rt,krw->ktw", home_map, flat_back, preferred_element_type=jnp.float32
    ).astype(jnp.bfloat16)
    return (gathered_home[0], gathered_home[1], gate_grad, up_grad, down_grad)


def solution(mesh):
    return jax.shard_map(
        body,
        mesh=mesh,
        in_specs=(
            P("expert", "tensor"),
            P("expert", None),
            P("expert"),
            P(),
            P("expert", "tensor"),
            P("expert", None, "tensor"),
            P("expert", None, "tensor"),
            P("expert", "tensor", None),
        ),
        out_specs=(
            P("expert", "tensor"),
            P("expert", "tensor"),
            P("expert", None, "tensor"),
            P("expert", None, "tensor"),
            P("expert", "tensor", None),
        ),
        check_vma=False,
    )
```

profile of v0, /device:TPU:1, one launch (start us, length us, event | category | flops | bytes accessed | tf_op | source)
XLA Modules:
  0.0 302.7 jit_solution(17173675187760145169)
XLA Ops:
  7.2 0.9 select_reduce_fusion
  8.1 1.0 fusion.24
  9.1 1.6 pad_maximum_fusion.1
  10.8 0.9 fusion.15
  11.7 28.7 %all-gather.2.cloned.1.call-done = bf16[2,128,2048]{2,1,0:T(8,128)(2,1)} async-done(((bf16[2,128,512]{2,1,0:T(8,128)(2,1)}), bf16[2,128,2048]{2,1,0:T(8,128)(2,1)}) %all-gather.2.cloned.1.call-update) | async-done | bytes 1048592 | tf_op jit(solution)/shard_map/all_gather | solution.py:42
  40.4 2.5 convert_bitcast_fusion
  43.5 107.7 %all_to_all.10 = bf16[2,64,8,2048]{3,2,0,1:T(8,128)(2,1)S(1)} all-to-all(bf16[2,64,8,2048]{3,2,0,1:T(8,128)(2,1)S(1)} %copy.27), channel_id=1, replica_groups=mesh['expert'=64,'tensor'=4] {'expert'}, dimensions={1} | all-to-all | bytes 8388608 | tf_op jit(solution)/shard_map/all_to_all | solution.py:52
  151.3 1.2 fusion.12
  152.5 1.9 copy-done.5
  154.4 1.3 fusion.5
  155.7 1.6 multiply_convert_fusion.2
  157.3 1.3 fusion.10
  158.7 3.3 %add_bitcast_fusion = f32[64,8,2048]{2,1,0:T(8,128)} fusion(f32[512,2048]{1,0:T(8,128)S(1)} %fusion.10, bf16[512,512]{1,0:T(8,128)(2,1)S(1)} %get-tuple-element.27, bf16[1,2048,512]{2,1,0:T(8,128)(2,1)S(1)} %copy-done), kind=kOutput, calls=%fused_computation | convolution fusion | flops 1074790400 | bytes 11010048 | tf_op jit(solution)/shard_map/dot_general | solution.py:85
  162.0 4.8 %fusion.3 = f32[64,8,2048]{2,1,0:T(8,128)} fusion(bf16[1,512,2048]{2,1,0:T(8,128)(2,1)} %param.15, bf16[512,512]{1,0:T(8,128)(2,1)S(1)} %get-tuple-element.25), kind=kOutput, calls=%fused_computation.12 | convolution fusion | flops 1073741824 | bytes 6815744 | tf_op jit(solution)/shard_map/dot_general | solution.py:66
  166.9 40.1 %reduce-scatter.5.cloned.1.call-done = f32[64,8,512]{2,1,0:T(8,128)} async-done(((f32[64,8,2048]{2,1,0:T(8,128)}), f32[64,8,512]{2,1,0:T(8,128)}) %reduce-scatter.5.cloned.1.call-update) | async-done | bytes 1048592 | tf_op jit(solution)/shard_map/reduce_scatter | solution.py:90
  207.0 51.8 %reduce-scatter.3.cloned.1.call-done = f32[64,8,512]{2,1,0:T(8,128)} async-done(((f32[64,8,2048]{2,1,0:T(8,128)}), f32[64,8,512]{2,1,0:T(8,128)}) %reduce-scatter.3.cloned.1.call-update) | async-done | bytes 1048592 | tf_op jit(solution)/shard_map/reduce_scatter | solution.py:89
  258.8 2.8 broadcast_select_fusion
  262.4 2.3 collective-permute-done
  265.1 1.0 copy.28
  266.1 10.4 %all-to-all-start.1 = ((bf16[2,64,4,512]{3,2,0,1:T(4,128)(2,1)}), bf16[2,64,4,512]{3,2,0,1:T(4,128)(2,1)S(1)}, u32[]{:S(2)}, u32[]{:S(2)}) async-start(bf16[2,64,4,512]{3,2,0,1:T(4,128)(2,1)} %copy.28), calls=%async_computation.3 | async-start | bytes 1048576 | tf_op jit(solution)/shard_map/all_to_all | solution.py:97
  276.5 4.5 %fusion.2 = bf16[1,512,2048]{2,1,0:T(8,128)(2,1)} fusion(bf16[512,512]{1,0:T(8,128)(2,1)} %copy-done.9, bf16[2,64,8,2048]{3,2,0,1:T(8,128)(2,1)} %copy-done.1), kind=kOutput, calls=%fused_computation.7 | convolution fusion | flops 1074790400 | bytes 4718592 | tf_op jit(solution)/shard_map/dot_general | solution.py:80
  281.0 2.6 fusion
  283.7 2.6 fusion.1
  286.3 7.5 %all-to-all-done.1 = bf16[2,64,4,512]{3,2,0,1:T(4,128)(2,1)S(1)} async-done(((bf16[2,64,4,512]{3,2,0,1:T(4,128)(2,1)}), bf16[2,64,4,512]{3,2,0,1:T(4,128)(2,1)S(1)}, u32[]{:S(2)}, u32[]{:S(2)}) %all-to-all-start.1) | async-done | bytes 524320 | tf_op jit(solution)/shard_map/all_to_all | solution.py:97
  (42 shorter events, 4.3 us)
Async XLA Ops:
  7.2 148.5 %copy-start = (bf16[1,2048,512]{2,1,0:T(8,128)(2,1)S(1)}, bf16[1,2048,512]{2,1,0:T(8,128)(2,1)}, u32[]{:S(2)}) copy-start(bf16[1,2048,512]{2,1,0:T(8,128)(2,1)} %param.14) | copy-start | bytes 6291460
  7.2 33.2 %all-gather.2.cloned.1.call-start = ((), (), s32[]{:S(2)}) async-start(), calls=%async_computation.4 | async-start | bytes 1310720 | tf_op jit(solution)/shard_map/all_gather | solution.py:42
  10.8 196.2 %reduce-scatter.5.cloned.1.call-start = ((), (), s32[]{:S(2)}) async-start(), calls=%async_computation.6 | async-start | bytes 5242880 | tf_op jit(solution)/shard_map/reduce_scatter | solution.py:90
  43.5 107.7 %copy-start.6 = (bf16[1,2048,512]{2,1,0:T(8,128)(2,1)S(1)}, bf16[1,2048,512]{2,1,0:T(8,128)(2,1)}, u32[]{:S(2)}) copy-start(bf16[1,2048,512]{2,1,0:T(8,128)(2,1)} %param.13) | copy-start | bytes 6291460
  151.2 4.4 %copy-start.1 = (bf16[2,64,8,2048]{3,2,0,1:T(8,128)(2,1)}, bf16[2,64,8,2048]{3,2,0,1:T(8,128)(2,1)S(1)}, u32[]{:S(2)}) copy-start(bf16[2,64,8,2048]{3,2,0,1:T(8,128)(2,1)S(1)} %all_to_all.10) | copy-start | bytes 12582916
  151.2 3.1 %copy-start.5 = (bf16[1,512,2048]{2,1,0:T(8,128)(2,1)S(1)}, bf16[1,512,2048]{2,1,0:T(8,128)(2,1)}, u32[]{:S(2)}) copy-start(bf16[1,512,2048]{2,1,0:T(8,128)(2,1)} %param.15) | copy-start | bytes 6291460
  157.3 1.3 copy-start.7
  157.3 1.3 copy-start.10
  157.3 4.7 %copy-start.9 = (bf16[512,512]{1,0:T(8,128)(2,1)}, bf16[512,512]{1,0:T(8,128)(2,1)S(1)}, u32[]{:S(2)}) copy-start(bf16[512,512]{1,0:T(8,128)(2,1)S(1)} %get-tuple-element.25) | copy-start | bytes 1572868
  161.9 96.9 %reduce-scatter.3.cloned.1.call-start = ((), (), s32[]{:S(2)}) async-start(), calls=%async_computation.5 | async-start | bytes 5242880 | tf_op jit(solution)/shard_map/reduce_scatter | solution.py:89
  207.0 57.7 %copy-start.3 = (f32[64,8,512]{2,1,0:T(8,128)S(1)}, f32[64,8,512]{2,1,0:T(8,128)}, u32[]{:S(2)}) copy-start(f32[64,8,512]{2,1,0:T(8,128)} %reduce-scatter.5.cloned.1.call-done) | copy-start | bytes 3145732
  258.8 5.8 %copy-start.4 = (f32[64,8,512]{2,1,0:T(8,128)S(1)}, f32[64,8,512]{2,1,0:T(8,128)}, u32[]{:S(2)}) copy-start(f32[64,8,512]{2,1,0:T(8,128)} %reduce-scatter.3.cloned.1.call-done) | copy-start | bytes 3145732
  261.6 14.8 %copy-start.12 = (s32[128,1]{0,1:T(1,128)S(1)}, s32[128,1]{0,1:T(1,128)}, u32[]{:S(2)}) copy-start(s32[128,1]{0,1:T(1,128)} %param.9) | copy-start | bytes 1540
  261.7 3.0 collective-permute-start
  266.1 27.7 %all-to-all-start.1 = ((bf16[2,64,4,512]{3,2,0,1:T(4,128)(2,1)}), bf16[2,64,4,512]{3,2,0,1:T(4,128)(2,1)S(1)}, u32[]{:S(2)}, u32[]{:S(2)}) async-start(bf16[2,64,4,512]{3,2,0,1:T(4,128)(2,1)} %copy.28), calls=%async_computation.3 | async-start | bytes 1048576 | tf_op jit(solution)/shard_map/all_to_all | solution.py:97
  276.5 4.5 %copy-start.2 = (bf16[2,64,8,2048]{3,2,0,1:T(8,128)(2,1)S(1)}, bf16[2,64,8,2048]{3,2,0,1:T(8,128)(2,1)}, u32[]{:S(2)}) copy-start(bf16[2,64,8,2048]{3,2,0,1:T(8,128)(2,1)} %copy-done.1) | copy-start | bytes 12582916
  276.5 4.5 %copy-start.8 = (bf16[512,512]{1,0:T(8,128)(2,1)S(1)}, bf16[512,512]{1,0:T(8,128)(2,1)}, u32[]{:S(2)}) copy-start(bf16[512,512]{1,0:T(8,128)(2,1)} %copy-done.7) | copy-start | bytes 1572868
  281.0 2.6 copy-start.11
Sparse Core Ops, SparseCore 0:
  10.9 29.4 all-gather.1
  162.1 44.8 reduce-scatter.4
  209.7 49.0 reduce-scatter.2
where the time goes:
time: 303 us
  waiting for transfers between devices  130 us (43%)
  blocking collectives  108 us (36%)
  matrix products  27 us (9%)
  between operations  14 us (5%)
  starting transfers between devices  11.2 us (4%)
  other arithmetic  6.76 us (2%)
  local copies, waits for them, and re-layouts  5.46 us (2%)
    all_to_all x1, blocking collectives, body(): lax.all_to_all(outbound, 'expert', split_axis=1, concat_axis=1, tiled=True)  108 us
    reduce_scatter x1, waiting for transfers between devices, body(): lax.psum_scatter(out_part, 'tensor', scatter_dimension=2, tiled=True)  51.8 us
    reduce_scatter x1, waiting for transfers between devices, body(): lax.psum_scatter(input_part, 'tensor', scatter_dimension=2, tiled=True)  40.1 us
    all_gather x1, waiting for transfers between devices, body(): sources = lax.all_gather(sources, 'tensor', axis=2, tiled=True)  28.7 us
    all_to_all x1, starting transfers between devices, body(): lax.all_to_all(going_back, 'expert', split_axis=1, concat_axis=1, tiled=T...  10.4 us
    all_to_all x1, waiting for transfers between devices, body(): lax.all_to_all(going_back, 'expert', split_axis=1, concat_axis=1, tiled=T...  7.52 us
  transfers between devices with their start and end apart: 5, of which 5 were waited for; matrix products, arithmetic and copies ran while one was open for 5% of the time, Pallas kernels for 0%

commit v1 on v0

--- a/solution.py
+++ b/solution.py
@@ -1,9 +1,48 @@
+import functools
 import jax
 import jax.numpy as jnp
 from jax import lax
 from jax.sharding import PartitionSpec as P
 
 SPLIT = 2
+
+
+def cubes_close(inner_x, dev_axis, axis_k):
+    block_out, oldest, val2 = (
+        lax.axis_size(dev_axis),
+        lax.axis_index(dev_axis),
+        inner_x.shape[axis_k],
+    )
+    aux = lax.dynamic_update_slice_in_dim(
+        jnp.zeros(
+            [k * block_out if tick == axis_k else k for tick, k in enumerate(inner_x.shape)],
+            inner_x.dtype,
+        ),
+        inner_x,
+        oldest * val2,
+        axis=axis_k,
+    )
+    outer = res = inner_x
+    for dev_j in range(1, block_out // 2 + 1):
+        outer = lax.ppermute(
+            outer,
+            axis_name=dev_axis,
+            perm=[(tick, (tick + 1) % block_out) for tick in range(block_out)],
+        )
+        aux = lax.dynamic_update_slice_in_dim(
+            aux, outer, (oldest - dev_j) % block_out * val2, axis=axis_k
+        )
+        if 2 * dev_j < block_out:
+            res = lax.ppermute(
+                res, dev_axis, [(tick, (tick - 1) % block_out) for tick in range(block_out)]
+            )
+            aux = lax.dynamic_update_slice_in_dim(
+                aux, res, (oldest + dev_j) % block_out * val2, axis=axis_k
+            )
+    return aux
+
+
+zone_do = functools.partial(cubes_close, dev_axis="tensor", axis_k=2)
 
 
 def partner(value, axis, stride):
@@ -39,7 +78,7 @@
     slot_pos = jnp.sum(before * lab_hot, axis=1).astype(jnp.int32)
     target_row = lang_label * capacity + slot_pos
     sources = jnp.stack((tokens, grad_rows))
-    sources = lax.all_gather(sources, "tensor", axis=2, tiled=True)
+    sources = zone_do(sources)
     slot_ids = jnp.arange(n_expert * capacity, dtype=jnp.int32)
     dispatch_map = (slot_ids[:, None] // capacity // SPLIT == lang_label[None, :]) & (
         slot_ids[:, None] % capacity == slot_pos[None, :]

time: 303 us -> 292 us (0.964)
  waiting for transfers between devices: 130 us -> 108 us
  starting transfers between devices: 11.2 us -> 16.7 us
  blocking collectives: 108 us -> 113 us
    all_gather x1 -> x0, waiting for transfers between devices: 28.7 us -> none  [body(): sources = lax.all_gather(sources, 'tensor', axis=2, tiled=True)]
    ppermute x0 -> x3, waiting for transfers between devices: none -> 8.06 us  [the longest x2 8.05 us: cubes_close(): lax.ppermute(outer, axis_name=dev_axis, perm=[(tick, (tick + 1) % block_o...]
    ppermute x0 -> x3, starting transfers between devices: none -> 5.28 us  [the longest x2 4.01 us: cubes_close(): lax.ppermute(outer, axis_name=dev_axis, perm=[(tick, (tick + 1) % block_o...]
    all_to_all x1, blocking collectives: 108 us -> 113 us  [body(): lax.all_to_all(outbound, 'expert', split_axis=1, concat_axis=1, tiled=True)]
  transfers between devices with their start and end apart: 5 -> 7, of which waited for: 5 -> 6; matrix products, arithmetic and copies ran while one was open for 5% -> 5% of each run, Pallas kernels for 0% -> 0%
where the time goes in v1:
time: 292 us; the launch traced here: 291 us
  blocking collectives  113 us (39%)
  waiting for transfers between devices  108 us (37%)
  matrix products  25.1 us (9%)
  starting transfers between devices  16.7 us (6%)
  between operations  14.3 us (5%)
  local copies, waits for them, and re-layouts  7.53 us (3%)
  other arithmetic  6.78 us (2%)
    all_to_all x1, blocking collectives, body(): lax.all_to_all(outbound, 'expert', split_axis=1, concat_axis=1, tiled=True)  113 us
    reduce_scatter x1, waiting for transfers between devices, body(): lax.psum_scatter(out_part, 'tensor', scatter_dimension=2, tiled=True)  51.8 us
    reduce_scatter x1, waiting for transfers between devices, body(): lax.psum_scatter(input_part, 'tensor', scatter_dimension=2, tiled=True)  38.6 us
    all_to_all x1, starting transfers between devices, body(): lax.all_to_all(going_back, 'expert', split_axis=1, concat_axis=1, tiled=T...  10.4 us
    ppermute x2, waiting for transfers between devices, cubes_close(): lax.ppermute(outer, axis_name=dev_axis, perm=[(tick, (tick + 1) % block_o...  8.05 us
    all_to_all x1, waiting for transfers between devices, body(): lax.all_to_all(going_back, 'expert', split_axis=1, concat_axis=1, tiled=T...  7.53 us
  transfers between devices with their start and end apart: 7, of which 6 were waited for; matrix products, arithmetic and copies ran while one was open for 5% of the time, Pallas kernels for 0%

profile of v1, /device:TPU:1, one launch (start us, length us, event | category | flops | bytes accessed | tf_op | source)
XLA Modules:
  0.0 291.4 jit_solution(10145970223390497946)
XLA Ops:
  9.3 1.7 pad_maximum_fusion.1
  10.9 2.0 collective-permute-start
  13.0 1.3 collective-permute-start.1
  14.4 3.8 %collective-permute-done = bf16[2,128,512]{2,1,0:T(8,128)(2,1)S(1)} collective-permute-done((bf16[2,128,512]{2,1,0:T(8,128)(2,1)}, bf16[2,128,512]{2,1,0:T(8,128)(2,1)S(1)}, u32[]{:S(2)}, u32[]{:S(2)}) %collective-permute-start) | collective-permute-done | bytes 262176 | tf_op jit(solution)/shard_map/ppermute | solution.py:27
  18.2 2.0 collective-permute-start.2
  21.2 4.2 %collective-permute-done.2 = bf16[2,128,512]{2,1,0:T(8,128)(2,1)} collective-permute-done((bf16[2,128,512]{2,1,0:T(8,128)(2,1)S(1)}, bf16[2,128,512]{2,1,0:T(8,128)(2,1)}, u32[]{:S(2)}, u32[]{:S(2)}) %collective-permute-start.2) | collective-permute-done | bytes 262176 | tf_op jit(solution)/shard_map/ppermute | solution.py:27
  26.5 1.3 convert_bitcast_fusion
  28.4 112.7 %all_to_all.10 = bf16[2,64,8,2048]{3,2,0,1:T(8,128)(2,1)S(1)} all-to-all(bf16[2,64,8,2048]{3,2,0,1:T(8,128)(2,1)S(1)} %copy.27), channel_id=1, replica_groups=mesh['expert'=64,'tensor'=4] {'expert'}, dimensions={1} | all-to-all | bytes 8388608 | tf_op jit(solution)/shard_map/all_to_all | solution.py:91
  141.0 1.2 fusion.12
  142.3 1.9 copy-done.5
  144.2 1.3 fusion.5
  145.5 1.6 multiply_convert_fusion.2
  147.1 1.3 fusion.10
  148.4 3.3 %add_bitcast_fusion = f32[64,8,2048]{2,1,0:T(8,128)} fusion(f32[512,2048]{1,0:T(8,128)S(1)} %fusion.10, bf16[512,512]{1,0:T(8,128)(2,1)S(1)} %get-tuple-element.27, bf16[1,2048,512]{2,1,0:T(8,128)(2,1)S(1)} %copy-done), kind=kOutput, calls=%fused_computation | convolution fusion | flops 1074790400 | bytes 11010048 | tf_op jit(solution)/shard_map/dot_general | solution.py:124
  152.0 4.8 %fusion.3 = f32[64,8,2048]{2,1,0:T(8,128)} fusion(bf16[1,512,2048]{2,1,0:T(8,128)(2,1)} %param.15, bf16[512,512]{1,0:T(8,128)(2,1)S(1)} %get-tuple-element.25), kind=kOutput, calls=%fused_computation.12 | convolution fusion | flops 1073741824 | bytes 6815744 | tf_op jit(solution)/shard_map/dot_general | solution.py:105
  156.8 38.6 %reduce-scatter.5.cloned.1.call-done = f32[64,8,512]{2,1,0:T(8,128)} async-done(((f32[64,8,2048]{2,1,0:T(8,128)}), f32[64,8,512]{2,1,0:T(8,128)}) %reduce-scatter.5.cloned.1.call-update) | async-done | bytes 1048592 | tf_op jit(solution)/shard_map/reduce_scatter | solution.py:129
  195.4 51.8 %reduce-scatter.3.cloned.1.call-done = f32[64,8,512]{2,1,0:T(8,128)} async-done(((f32[64,8,2048]{2,1,0:T(8,128)}), f32[64,8,512]{2,1,0:T(8,128)}) %reduce-scatter.3.cloned.1.call-update) | async-done | bytes 1048592 | tf_op jit(solution)/shard_map/reduce_scatter | solution.py:128
  247.3 2.8 broadcast_select_fusion
  250.8 2.3 collective-permute-done.3
  254.5 10.4 %all-to-all-start.1 = ((bf16[2,64,4,512]{3,2,0,1:T(4,128)(2,1)}), bf16[2,64,4,512]{3,2,0,1:T(4,128)(2,1)S(1)}, u32[]{:S(2)}, u32[]{:S(2)}) async-start(bf16[2,64,4,512]{3,2,0,1:T(4,128)(2,1)} %copy.28), calls=%async_computation.3 | async-start | bytes 1048576 | tf_op jit(solution)/shard_map/all_to_all | solution.py:136
  264.9 4.5 %fusion.2 = bf16[1,512,2048]{2,1,0:T(8,128)(2,1)} fusion(bf16[512,512]{1,0:T(8,128)(2,1)} %copy-done.9, bf16[2,64,8,2048]{3,2,0,1:T(8,128)(2,1)} %copy-done.1), kind=kOutput, calls=%fused_computation.7 | convolution fusion | flops 1074790400 | bytes 4718592 | tf_op jit(solution)/shard_map/dot_general | solution.py:119
  269.4 2.6 fusion
  272.1 2.6 fusion.1
  274.7 7.5 %all-to-all-done.1 = bf16[2,64,4,512]{3,2,0,1:T(4,128)(2,1)S(1)} async-done(((bf16[2,64,4,512]{3,2,0,1:T(4,128)(2,1)}), bf16[2,64,4,512]{3,2,0,1:T(4,128)(2,1)S(1)}, u32[]{:S(2)}, u32[]{:S(2)}) %all-to-all-start.1) | async-done | bytes 524320 | tf_op jit(solution)/shard_map/all_to_all | solution.py:136
  (49 shorter events, 9.5 us)
Async XLA Ops:
  7.2 138.3 %copy-start = (bf16[1,2048,512]{2,1,0:T(8,128)(2,1)S(1)}, bf16[1,2048,512]{2,1,0:T(8,128)(2,1)}, u32[]{:S(2)}) copy-start(bf16[1,2048,512]{2,1,0:T(8,128)(2,1)} %param.14) | copy-start | bytes 6291460
  7.2 7.0 %copy-start.12 = (s32[128,1]{0,1:T(1,128)S(1)}, s32[128,1]{0,1:T(1,128)}, u32[]{:S(2)}) copy-start(s32[128,1]{0,1:T(1,128)} %param.9) | copy-start | bytes 1540
  7.2 188.2 %reduce-scatter.5.cloned.1.call-start = ((), (), s32[]{:S(2)}) async-start(), calls=%async_computation.5 | async-start | bytes 5242880 | tf_op jit(solution)/shard_map/reduce_scatter | solution.py:129
  10.9 7.3 %collective-permute-start = (bf16[2,128,512]{2,1,0:T(8,128)(2,1)}, bf16[2,128,512]{2,1,0:T(8,128)(2,1)S(1)}, u32[]{:S(2)}, u32[]{:S(2)}) collective-permute-start(bf16[2,128,512]{2,1,0:T(8,128)(2,1)} %get-tuple-element.30), channel_id=1, source_target_pairs={{0,1},{1,2},{2,3},{3,0},{4,5},{5,6},{6,7},{7,4},{8,9},{9,10},{10,1... | collective-permute-start | bytes 786440 | tf_op jit(solution)/shard_map/ppermute | solution.py:27
  13.0 7.3 %collective-permute-start.1 = (bf16[2,128,512]{2,1,0:T(8,128)(2,1)}, bf16[2,128,512]{2,1,0:T(8,128)(2,1)}, u32[]{:S(2)}, u32[]{:S(2)}) collective-permute-start(bf16[2,128,512]{2,1,0:T(8,128)(2,1)} %get-tuple-element.30), channel_id=1, source_target_pairs={{0,3},{1,0},{2,1},{3,2},{4,7},{5,4},{6,5},{7,6},{8,11},{9,8},{10,9... | collective-permute-start | bytes 786440 | tf_op jit(solution)/shard_map/ppermute | solution.py:36
  18.2 7.3 %collective-permute-start.2 = (bf16[2,128,512]{2,1,0:T(8,128)(2,1)S(1)}, bf16[2,128,512]{2,1,0:T(8,128)(2,1)}, u32[]{:S(2)}, u32[]{:S(2)}) collective-permute-start(bf16[2,128,512]{2,1,0:T(8,128)(2,1)S(1)} %collective-permute-done), channel_id=1, source_target_pairs={{0,1},{1,2},{2,3},{3,0},{4,5},{5,6},{6,7},{7,4},{8,9},{9,10},{10,1... | collective-permute-start | bytes 786440 | tf_op jit(solution)/shard_map/ppermute | solution.py:27
  28.4 112.7 %copy-start.6 = (bf16[1,2048,512]{2,1,0:T(8,128)(2,1)S(1)}, bf16[1,2048,512]{2,1,0:T(8,128)(2,1)}, u32[]{:S(2)}) copy-start(bf16[1,2048,512]{2,1,0:T(8,128)(2,1)} %param.13) | copy-start | bytes 6291460
  141.0 4.4 %copy-start.1 = (bf16[2,64,8,2048]{3,2,0,1:T(8,128)(2,1)}, bf16[2,64,8,2048]{3,2,0,1:T(8,128)(2,1)S(1)}, u32[]{:S(2)}) copy-start(bf16[2,64,8,2048]{3,2,0,1:T(8,128)(2,1)S(1)} %all_to_all.10) | copy-start | bytes 12582916
  141.0 3.1 %copy-start.5 = (bf16[1,512,2048]{2,1,0:T(8,128)(2,1)S(1)}, bf16[1,512,2048]{2,1,0:T(8,128)(2,1)}, u32[]{:S(2)}) copy-start(bf16[1,512,2048]{2,1,0:T(8,128)(2,1)} %param.15) | copy-start | bytes 6291460
  147.1 1.3 copy-start.7
  147.1 1.3 copy-start.10
  147.1 4.8 %copy-start.9 = (bf16[512,512]{1,0:T(8,128)(2,1)}, bf16[512,512]{1,0:T(8,128)(2,1)S(1)}, u32[]{:S(2)}) copy-start(bf16[512,512]{1,0:T(8,128)(2,1)S(1)} %get-tuple-element.25) | copy-start | bytes 1572868
  151.7 95.5 %reduce-scatter.3.cloned.1.call-start = ((), (), s32[]{:S(2)}) async-start(), calls=%async_computation.4 | async-start | bytes 5242880 | tf_op jit(solution)/shard_map/reduce_scatter | solution.py:128
  195.4 57.7 %copy-start.3 = (f32[64,8,512]{2,1,0:T(8,128)S(1)}, f32[64,8,512]{2,1,0:T(8,128)}, u32[]{:S(2)}) copy-start(f32[64,8,512]{2,1,0:T(8,128)} %reduce-scatter.5.cloned.1.call-done) | copy-start | bytes 3145732
  247.3 5.8 %copy-start.4 = (f32[64,8,512]{2,1,0:T(8,128)S(1)}, f32[64,8,512]{2,1,0:T(8,128)}, u32[]{:S(2)}) copy-start(f32[64,8,512]{2,1,0:T(8,128)} %reduce-scatter.3.cloned.1.call-done) | copy-start | bytes 3145732
  250.1 3.0 %collective-permute-start.3 = (f32[2,64,4,512]{3,2,1,0:T(4,128)S(1)}, f32[2,64,4,512]{3,2,1,0:T(4,128)S(1)}, u32[]{:S(2)}, u32[]{:S(2)}) collective-permute-start(f32[2,64,4,512]{3,2,1,0:T(4,128)S(1)} %broadcast_select_fusion), channel_id=1, source_target_pairs={{0,4},{4,0},{8,12},{12,8},{16,20},{20,16},{24,28},{28,24},{32,36},... | collective-permute-start | bytes 3145736 | tf_op jit(solution)/shard_map/ppermute | solution.py:49
  254.5 27.7 %all-to-all-start.1 = ((bf16[2,64,4,512]{3,2,0,1:T(4,128)(2,1)}), bf16[2,64,4,512]{3,2,0,1:T(4,128)(2,1)S(1)}, u32[]{:S(2)}, u32[]{:S(2)}) async-start(bf16[2,64,4,512]{3,2,0,1:T(4,128)(2,1)} %copy.28), calls=%async_computation.3 | async-start | bytes 1048576 | tf_op jit(solution)/shard_map/all_to_all | solution.py:136
  264.9 4.5 %copy-start.2 = (bf16[2,64,8,2048]{3,2,0,1:T(8,128)(2,1)S(1)}, bf16[2,64,8,2048]{3,2,0,1:T(8,128)(2,1)}, u32[]{:S(2)}) copy-start(bf16[2,64,8,2048]{3,2,0,1:T(8,128)(2,1)} %copy-done.1) | copy-start | bytes 12582916
  264.9 4.5 %copy-start.8 = (bf16[512,512]{1,0:T(8,128)(2,1)S(1)}, bf16[512,512]{1,0:T(8,128)(2,1)}, u32[]{:S(2)}) copy-start(bf16[512,512]{1,0:T(8,128)(2,1)} %copy-done.7) | copy-start | bytes 1572868
  269.4 2.6 copy-start.11
Sparse Core Ops, SparseCore 0:
  151.9 43.5 reduce-scatter.4
  198.1 49.0 reduce-scatter.2
